TPU v7x, 512 devices: a whole 4x4x16 slice. The times are simulated.
512 devices in a mesh: req: 128 (over z, y, core), tp: 4 (over x).
Axes of the slice: x: 4, y: 4, z: 16, core: 2. Of those that a mesh axis runs over, the one named last changes fastest.
Arguments:
- states: bfloat16 [32768, 3072], P('req', 'tp'), may hold values from -12 to 12
- query_weight: bfloat16 [3072, 1536], P(None, 'tp'), may hold values from -0.75 to 0.75
- key_value_weight: bfloat16 [3072, 512], P(None, 'tp'), may hold values from -0.75 to 0.75
- lengths: int32 [128], P('req'), may hold values from 1 to 256, 16384 in all
- adapter_ids: int32 [128], P('req'), may hold values from 0 to 63, as said below
- adapter_slot: int32 [64], replicated, may hold values from 0 to 127, as said below
- down_store: bfloat16 [128, 3072, 32], P('req', 'tp'), may hold values from -0.109375 to 0.109375
- query_up_store: bfloat16 [128, 16, 1536], P('req', None, 'tp'), may hold values from -1.5 to 1.5
- key_value_store: bfloat16 [128, 16, 512], P('req', None, 'tp'), may hold values from -1.5 to 1.5
Outputs:
- context: bfloat16 [32768, 1536], P('req', 'tp')
Inputs may be any that keep to these rules, and one draw needn't show every extreme that they name: `adapter_ids`: exactly 16 distinct adapters are named among all 128 requests. `adapter_slot`: distinct adapters have distinct rows.
All inputs are finite; a program needn't handle non-finite values. No bound on the sum of `lengths` on one device may be relied on, other than what follows from the above.
Results may differ from a plain program's by a relative error of at most 0.0072.
Values may be sent and summed in bfloat16 or wider, within the bound.
No kernel may reach another device: no remote copies, remote signals or barrier semaphores. Data moves between devices by JAX's collectives and lax.ppermute only.
A program may use at most 64 MiB of HBM per device.

v0:
```python
import math
import jax
import jax.numpy as jnp
from jax import lax
from jax.sharding import PartitionSpec as P

HEADS = 12
HEAD_DIM = 128
adapter_scale = 0.5
rope_base = 100000000000.0


def rotate(field):
    half = field.shape[-1] // 2
    count = field.shape[-3]
    position = jnp.arange(count).astype(jnp.float32)
    inverse = rope_base ** (-(jnp.arange(half).astype(jnp.float32) * 2.0) / field.shape[-1])
    angle = position[:, None] * inverse[None, :]
    cosine = jnp.cos(angle)[:, None, :]
    sine = jnp.sin(angle)[:, None, :]
    first_half = field[..., :half]
    second_half = field[..., half:]
    return jnp.concatenate(
        [first_half * cosine - second_half * sine, second_half * cosine + first_half * sine],
        axis=-1,
    )


def lookup_slots(wanted, adapter_slot):
    table = jnp.arange(adapter_slot.shape[0], dtype=jnp.int32)
    matches = wanted[:, None] == table[None, :]
    return jnp.sum(jnp.where(matches, adapter_slot[None, :], 0), axis=1)


def local(
    states,
    query_weight,
    key_value_weight,
    lengths,
    adapter_ids,
    adapter_slot,
    down_store,
    query_up_store,
    key_value_store,
):
    tp_index = lax.axis_index("tp")
    req_dev = lengths.shape[0]
    rows_total = states.shape[0]
    slot_len = rows_total // req_dev
    q_cols = query_weight.shape[1]
    kv_cols = key_value_weight.shape[1]
    heads_here = q_cols // HEAD_DIM
    pooled = (
        lax.all_gather(down_store, "req", axis=0, tiled=True),
        lax.all_gather(query_up_store, "req", axis=0, tiled=True),
        lax.all_gather(key_value_store, "req", axis=0, tiled=True),
    )
    own_slots = lookup_slots(adapter_ids, adapter_slot)
    adapter_down, adapter_query, adapter_pair = (
        jnp.take(member, own_slots, axis=0) for member in pooled
    )
    full_down = lax.all_gather(adapter_down, "tp", axis=1, tiled=True)
    piece = lax.all_gather(states, "tp", axis=1, tiled=True)
    width = piece.shape[1]
    grouped = piece.reshape(req_dev, slot_len, width)
    query_total = jnp.dot(piece, query_weight, preferred_element_type=jnp.float32)
    key_value_sum = jnp.dot(piece, key_value_weight, preferred_element_type=jnp.float32)
    rank_sum = jnp.einsum("rsd,rdk->rsk", grouped, full_down, preferred_element_type=jnp.float32)
    rank_mid = rank_sum.astype(jnp.bfloat16)
    rank_cols = rank_mid.shape[2] // 2
    query_addition = jnp.einsum(
        "rsk,rkc->rsc",
        rank_mid[:, :, :rank_cols],
        adapter_query,
        preferred_element_type=jnp.float32,
    ).reshape(rows_total, q_cols)
    key_value_extra = jnp.einsum(
        "rsk,rkc->rsc", rank_mid[:, :, rank_cols:], adapter_pair, preferred_element_type=jnp.float32
    ).reshape(rows_total, kv_cols)
    query_plain = query_total + adapter_scale * query_addition
    key_value_own = (key_value_sum + adapter_scale * key_value_extra).astype(jnp.bfloat16)
    pair_all = lax.all_gather(key_value_own, "tp", axis=1, tiled=True)
    key_width = pair_all.shape[1] // 2
    kv_heads = key_width // HEAD_DIM
    group = HEADS // kv_heads
    kv_index = tp_index * heads_here // group
    key_block = lax.dynamic_slice_in_dim(pair_all, kv_index * HEAD_DIM, HEAD_DIM, 1)
    value_block = lax.dynamic_slice_in_dim(pair_all, key_width + kv_index * HEAD_DIM, HEAD_DIM, 1)
    queries = rotate(query_plain.reshape(req_dev, slot_len, heads_here, HEAD_DIM)).astype(
        jnp.bfloat16
    )
    keys_one = rotate(key_block.astype(jnp.float32).reshape(req_dev, slot_len, 1, HEAD_DIM)).astype(
        jnp.bfloat16
    )[:, :, 0, :]
    values_one = value_block.reshape(req_dev, slot_len, HEAD_DIM)
    scale = 1.0 / math.sqrt(HEAD_DIM)
    scores = (
        jnp.einsum("rqhd,rkd->rhqk", queries, keys_one, preferred_element_type=jnp.float32) * scale
    )
    position = jnp.arange(slot_len, dtype=jnp.int32)
    allowed = (position[None, None, :] <= position[None, :, None]) & (
        position[None, None, :] < lengths[:, None, None]
    )
    scores = jnp.where(allowed[:, None, :, :], scores, -jnp.inf)
    highest = jnp.max(scores, axis=-1, keepdims=True)
    expo = jnp.exp(scores - highest)
    weights = (expo / jnp.sum(expo, axis=-1, keepdims=True)).astype(jnp.bfloat16)
    context = jnp.einsum("rhqk,rkd->rqhd", weights, values_one, preferred_element_type=jnp.float32)
    live_rows = position[None, :] < lengths[:, None]
    context = jnp.where(live_rows[:, :, None, None], context, 0.0)
    return context.reshape(rows_total, q_cols).astype(jnp.bfloat16)


def solution(mesh):
    return jax.shard_map(
        local,
        mesh=mesh,
        in_specs=(
            P("req", "tp"),
            P(None, "tp"),
            P(None, "tp"),
            P("req"),
            P("req"),
            P(),
            P("req", "tp", None),
            P("req", None, "tp"),
            P("req", None, "tp"),
        ),
        out_specs=P("req", "tp"),
        check_vma=False,
    )
```

profile of v0, /device:TPU:2, one launch (start us, length us, event | category | flops | bytes accessed | tf_op | source)
XLA Modules:
  0.0 358.5 jit_solution(2716103049818812552)
XLA Ops:
  6.5 0.0 copy-start
  6.5 0.0 all-gather.4.cloned.1.call-start
  6.5 0.7 all-gather.4.cloned.1.call-update
  7.3 0.0 all-gather.6.cloned.1.call-start
  7.3 0.7 all-gather.6.cloned.1.call-update
  8.0 0.0 all-gather.8.cloned.1.call-start
  8.1 0.7 all-gather.8.cloned.1.call-update
  9.4 1.3 fusion.39
  13.3 0.0 copy-start.4
  13.4 0.0 copy-start.6
  13.4 0.0 copy-start.2
  13.4 96.3 %all_gather.21 = bf16[128,16,128]{2,1,0:T(8,128)(2,1)} all-gather(bf16[1,16,128]{2,1,0:T(8,128)(2,1)} %param.17), channel_id=1, replica_groups=mesh['req'=128,'tp'=4] {'req'}, dimensions={0}, use_global_device_ids=true | all-gather | bytes 528384 | tf_op jit(solution)/shard_map/all_gather | solution.py:56
  109.7 0.0 copy-done.6
  109.7 0.1 fusion.9
  109.8 0.0 copy-done.4
  109.8 0.0 copy-done.2
  109.8 1.2 multiply_cosine_fusion
  111.0 0.0 all-gather.4.cloned.1.call-done
  111.0 0.0 copy-done
  111.0 2.4 fusion.45
  113.4 82.7 %all-gather.6.cloned.1.call-done = bf16[128,768,32]{1,2,0:T(8,128)(2,1)} async-done(((bf16[1,768,32]{1,2,0:T(8,128)(2,1)}), bf16[128,768,32]{1,2,0:T(8,128)(2,1)}) %all-gather.6.cloned.1.call-update) | async-done | bytes 6291472 | tf_op jit(solution)/shard_map/all_gather | solution.py:54
  196.1 0.8 dynamic-slice_select_fusion
  196.9 12.4 %all_gather.20 = bf16[1,3072,32]{1,2,0:T(8,128)(2,1)S(1)} all-gather(bf16[1,768,32]{1,2,0:T(8,128)(2,1)S(1)} %dynamic-slice_select_fusion), channel_id=1, replica_groups=mesh['req'=128,'tp'=4] {'tp'}, dimensions={1}, use_global_device_ids=true | all-gather | bytes 245760 | tf_op jit(solution)/shard_map/all_gather | solution.py:62
  209.3 2.0 fusion.6
  211.2 121.7 %all-gather.8.cloned.1.call-done = bf16[128,16,384]{2,1,0:T(8,128)(2,1)} async-done(((bf16[1,16,384]{2,1,0:T(8,128)(2,1)}), bf16[128,16,384]{2,1,0:T(8,128)(2,1)}) %all-gather.8.cloned.1.call-update) | async-done | bytes 1572880 | tf_op jit(solution)/shard_map/all_gather | solution.py:55
  332.9 1.0 fusion.2
  333.9 0.2 copy.21
  334.1 0.2 copy.30
  334.3 0.2 copy.31
  334.4 0.9 convolution_multiply_fusion.2
  335.3 0.0 copy-start.3
  335.3 0.0 copy-start.5
  335.4 0.0 copy-start.1
  335.4 2.2 fusion.5
  337.6 12.0 %all_gather.22 = bf16[256,512]{1,0:T(8,128)(2,1)S(1)} all-gather(bf16[256,128]{1,0:T(8,128)(2,1)S(1)} %fusion.5), channel_id=1, replica_groups=mesh['req'=128,'tp'=4] {'tp'}, dimensions={1}, use_global_device_ids=true | all-gather | bytes 327680 | tf_op jit(solution)/shard_map/all_gather | solution.py:82
  349.6 0.0 copy-done.3
  349.6 0.0 copy-done.5
  349.6 0.6 fusion.29
  350.2 0.0 copy-done.1
  350.2 0.0 copy-start.7
  350.2 0.1 fusion.10
  350.4 0.4 fusion.44
  350.7 0.1 fusion.7
  350.9 0.0 copy-done.7
  350.9 0.3 fusion.4
  351.2 0.8 copy.26
  (5 shorter events, 0.1 us)
Async XLA Ops:
  6.5 104.5 %copy-start = (bf16[3072,384]{1,0:T(8,128)(2,1)S(1)}, bf16[3072,384]{1,0:T(8,128)(2,1)}, u32[]{:S(2)}) copy-start(bf16[3072,384]{1,0:T(8,128)(2,1)} %param.10) | copy-start | bytes 7077892
  6.5 104.5 %all-gather.4.cloned.1.call-start = ((), (), s32[]{:S(2)}) async-start(), calls=%async_computation | async-start | bytes 1966080 | tf_op jit(solution)/shard_map/all_gather | solution.py:63
  7.3 188.8 %all-gather.6.cloned.1.call-start = ((), (), s32[]{:S(2)}) async-start(), calls=%async_computation.1 | async-start | bytes 6340608 | tf_op jit(solution)/shard_map/all_gather | solution.py:54
  8.0 324.9 %all-gather.8.cloned.1.call-start = ((), (), s32[]{:S(2)}) async-start(), calls=%async_computation.2 | async-start | bytes 1585152 | tf_op jit(solution)/shard_map/all_gather | solution.py:55
  13.3 96.5 %copy-start.4 = (f32[64]{0:T(128)}, f32[64]{0:T(128)S(1)}, u32[]{:S(2)}) copy-start(f32[64]{0:T(128)S(1)} %multiply_power_fusion) | copy-start | bytes 772
  13.4 96.3 %copy-start.6 = (pred[256]{0:T(512)(128)(4,1)}, pred[256]{0:T(512)(128)(4,1)S(1)}, u32[]{:S(2)}) copy-start(pred[256]{0:T(512)(128)(4,1)S(1)} %iota_compare_fusion.1) | copy-start | bytes 772
  13.4 96.4 %copy-start.2 = (f32[256]{0:T(256)}, f32[256]{0:T(256)S(1)}, u32[]{:S(2)}) copy-start(f32[256]{0:T(256)S(1)} %iota_convert_fusion) | copy-start | bytes 3076
  335.3 14.3 %copy-start.3 = (f32[256]{0:T(256)S(1)}, f32[256]{0:T(256)}, u32[]{:S(2)}) copy-start(f32[256]{0:T(256)} %copy-done.2) | copy-start | bytes 3076
  335.3 14.3 %copy-start.5 = (f32[64]{0:T(128)S(1)}, f32[64]{0:T(128)}, u32[]{:S(2)}) copy-start(f32[64]{0:T(128)} %copy-done.4) | copy-start | bytes 772
  335.4 14.9 %copy-start.1 = (f32[256,64]{1,0:T(8,128)S(1)}, f32[256,64]{1,0:T(8,128)}, u32[]{:S(2)}) copy-start(f32[256,64]{1,0:T(8,128)} %get-tuple-element.45) | copy-start | bytes 196612
  350.2 0.7 copy-start.7
Sparse Core Ops, SparseCore 0:
  9.5 37.5 all-gather.3
  50.2 145.7 all-gather.5
  199.1 133.7 all-gather.7
where the time goes:
time: 359 us
  waiting for transfers between devices  206 us (57%)
  blocking collectives  121 us (34%)
  between operations  16.5 us (5%)
  matrix products  9.02 us (3%)
  other arithmetic  4.29 us (1%)
    all_gather x1, waiting for transfers between devices, local(): lax.all_gather(query_up_store, 'req', axis=0, tiled=True)  122 us
    all_gather x1, blocking collectives, local(): lax.all_gather(key_value_store, 'req', axis=0, tiled=True)  96.3 us
    all_gather x1, waiting for transfers between devices, local(): lax.all_gather(down_store, 'req', axis=0, tiled=True)  82.7 us
    all_gather x1, blocking collectives, local(): full_down = lax.all_gather(adapter_down, 'tp', axis=1, tiled=True)  12.4 us
    all_gather x1, blocking collectives, local(): pair_all = lax.all_gather(key_value_own, 'tp', axis=1, tiled=True)  12 us
  transfers between devices with their start and end apart: 3, of which 2 were waited for; matrix products, arithmetic and copies ran while one was open for 2% of the time, Pallas kernels for 0%

commit v1 on v0

--- a/solution.py
+++ b/solution.py
@@ -79,7 +79,12 @@
     ).reshape(rows_total, kv_cols)
     query_plain = query_total + adapter_scale * query_addition
     key_value_own = (key_value_sum + adapter_scale * key_value_extra).astype(jnp.bfloat16)
-    pair_all = lax.all_gather(key_value_own, "tp", axis=1, tiled=True)
+    ring = [key_value_own]
+    for hop in range(3):
+        ring.append(lax.ppermute(ring[-1], "tp", [(dev, (dev + 1) % 4) for dev in range(4)]))
+    pair_all = jnp.roll(
+        jnp.concatenate(ring[::-1], axis=1), (lax.axis_index("tp") + 1) * ring[0].shape[1], axis=1
+    )
     key_width = pair_all.shape[1] // 2
     kv_heads = key_width // HEAD_DIM
     group = HEADS // kv_heads

time: 359 us -> 361 us (level)
  the two profiles are of different devices: /device:TPU:2 before, /device:TPU:1 now
where the time goes in v1:
time: 361 us
  waiting for transfers between devices  210 us (58%)
  blocking collectives  108 us (30%)
  between operations  16.5 us (5%)
  matrix products  8.68 us (2%)
  starting transfers between devices  7.33 us (2%)
  other arithmetic  5.65 us (2%)
  local copies, waits for them, and re-layouts  4.76 us (1%)
    all_gather x1, waiting for transfers between devices, local(): lax.all_gather(query_up_store, 'req', axis=0, tiled=True)  120 us
    all_gather x1, blocking collectives, local(): lax.all_gather(key_value_store, 'req', axis=0, tiled=True)  97.6 us
    all_gather x1, waiting for transfers between devices, local(): lax.all_gather(down_store, 'req', axis=0, tiled=True)  81.3 us
    all_gather x1, blocking collectives, local(): full_down = lax.all_gather(adapter_down, 'tp', axis=1, tiled=True)  10.1 us
    ppermute x3, starting transfers between devices, local(): lax.ppermute(ring[-1], 'tp', [(dev, (dev + 1) % 4) for dev in range(4)])  7.25 us
  transfers between devices with their start and end apart: 6, of which 4 were waited for; matrix products, arithmetic and copies ran while one was open for 4% of the time, Pallas kernels for 0%

profile of v1, /device:TPU:1, one launch (start us, length us, event | category | flops | bytes accessed | tf_op | source)
XLA Modules:
  0.0 360.6 jit_solution(9821971737456508959)
XLA Ops:
  6.5 0.0 copy-start
  6.5 0.0 all-gather.4.cloned.1.call-start
  6.5 0.7 all-gather.4.cloned.1.call-update
  7.3 0.0 all-gather.6.cloned.1.call-start
  7.3 0.7 all-gather.6.cloned.1.call-update
  8.0 0.0 all-gather.8.cloned.1.call-start
  8.1 0.7 all-gather.8.cloned.1.call-update
  9.4 1.3 fusion.39
  13.3 97.6 %all_gather.18 = bf16[128,16,128]{2,1,0:T(8,128)(2,1)} all-gather(bf16[1,16,128]{2,1,0:T(8,128)(2,1)} %param.17), channel_id=1, replica_groups=mesh['req'=128,'tp'=4] {'req'}, dimensions={0}, use_global_device_ids=true | all-gather | bytes 528384 | tf_op jit(solution)/shard_map/all_gather | solution.py:56
  110.9 0.7 fusion.9
  111.6 1.2 multiply_cosine_fusion
  112.8 0.0 all-gather.4.cloned.1.call-done
  112.8 0.0 copy-done
  112.8 0.0 copy-start.2
  112.8 3.2 fusion.45
  116.0 81.3 %all-gather.6.cloned.1.call-done = bf16[128,768,32]{1,2,0:T(8,128)(2,1)} async-done(((bf16[1,768,32]{1,2,0:T(8,128)(2,1)}), bf16[128,768,32]{1,2,0:T(8,128)(2,1)}) %all-gather.6.cloned.1.call-update) | async-done | bytes 6291472 | tf_op jit(solution)/shard_map/all_gather | solution.py:54
  197.3 0.0 copy-start.1
  197.3 0.9 dynamic-slice_select_fusion
  198.3 10.1 %all_gather.17 = bf16[1,3072,32]{1,2,0:T(8,128)(2,1)S(1)} all-gather(bf16[1,768,32]{1,2,0:T(8,128)(2,1)S(1)} %dynamic-slice_select_fusion), channel_id=1, replica_groups=mesh['req'=128,'tp'=4] {'tp'}, dimensions={1}, use_global_device_ids=true | all-gather | bytes 245760 | tf_op jit(solution)/shard_map/all_gather | solution.py:62
  208.4 2.0 fusion.6
  210.3 0.9 convolution_multiply_fusion.2
  211.2 0.0 copy-done.2
  211.3 0.0 copy-done.1
  211.3 0.7 fusion.5
  211.9 2.3 collective-permute-start
  214.2 120.0 %all-gather.8.cloned.1.call-done = bf16[128,16,384]{2,1,0:T(8,128)(2,1)} async-done(((bf16[1,16,384]{2,1,0:T(8,128)(2,1)}), bf16[128,16,384]{2,1,0:T(8,128)(2,1)}) %all-gather.8.cloned.1.call-update) | async-done | bytes 1572880 | tf_op jit(solution)/shard_map/all_gather | solution.py:55
  334.2 1.3 fusion.2
  335.5 0.2 copy.21
  335.7 0.0 collective-permute-done
  335.7 3.1 collective-permute-start.1
  338.8 0.2 copy.30
  339.0 0.2 copy.31
  339.2 0.0 copy-start.3
  339.2 3.0 collective-permute-done.1
  342.2 1.9 collective-permute-start.2
  344.1 1.0 fusion.10
  345.2 3.5 collective-permute-done.2
  348.6 0.8 constant_dynamic-update-slice_fusion.6
  349.5 0.8 constant_dynamic-update-slice_fusion.5
  350.4 0.8 constant_dynamic-update-slice_fusion.2
  351.2 0.8 constant_dynamic-update-slice_fusion.1
  352.1 0.3 fusion.29
  352.4 0.0 copy-done.3
  352.4 0.4 fusion.44
  352.8 0.1 fusion.7
  353.0 0.3 fusion.4
  353.2 0.8 copy.26
  (9 shorter events, 0.1 us)
Async XLA Ops:
  6.5 106.3 %copy-start = (bf16[3072,384]{1,0:T(8,128)(2,1)S(1)}, bf16[3072,384]{1,0:T(8,128)(2,1)}, u32[]{:S(2)}) copy-start(bf16[3072,384]{1,0:T(8,128)(2,1)} %param.10) | copy-start | bytes 7077892
  6.5 106.3 %all-gather.4.cloned.1.call-start = ((), (), s32[]{:S(2)}) async-start(), calls=%async_computation | async-start | bytes 1966080 | tf_op jit(solution)/shard_map/all_gather | solution.py:63
  7.3 190.1 %all-gather.6.cloned.1.call-start = ((), (), s32[]{:S(2)}) async-start(), calls=%async_computation.1 | async-start | bytes 6340608 | tf_op jit(solution)/shard_map/all_gather | solution.py:54
  8.0 326.2 %all-gather.8.cloned.1.call-start = ((), (), s32[]{:S(2)}) async-start(), calls=%async_computation.2 | async-start | bytes 1585152 | tf_op jit(solution)/shard_map/all_gather | solution.py:55
  112.8 98.4 %copy-start.2 = (bf16[3072,128]{1,0:T(8,128)(2,1)S(1)}, bf16[3072,128]{1,0:T(8,128)(2,1)}, u32[]{:S(2)}) copy-start(bf16[3072,128]{1,0:T(8,128)(2,1)} %param.11) | copy-start | bytes 2359300
  197.3 13.9 %copy-start.1 = (bf16[256,3072]{1,0:T(8,128)(2,1)S(1)}, bf16[256,3072]{1,0:T(8,128)(2,1)}, u32[]{:S(2)}) copy-start(bf16[256,3072]{1,0:T(8,128)(2,1)} %all-gather.4.cloned.1.call-done) | copy-start | bytes 4718596
  211.9 123.7 %collective-permute-start = (bf16[256,128]{0,1:T(8,128)(2,1)S(1)}, bf16[256,128]{0,1:T(8,128)(2,1)}, u32[]{:S(2)}, u32[]{:S(2)}) collective-permute-start(bf16[256,128]{0,1:T(8,128)(2,1)S(1)} %fusion.5), channel_id=1, source_target_pairs={{0,1},{1,2},{2,3},{3,0},{4,5},{5,6},{6,7},{7,4},{8,9},{9,10},{10,1... | collective-permute-start | bytes 196616 | tf_op jit(solution)/shard_map/ppermute | solution.py:84
  335.7 6.5 %collective-permute-start.1 = (bf16[256,128]{0,1:T(8,128)(2,1)}, bf16[256,128]{0,1:T(8,128)(2,1)}, u32[]{:S(2)}, u32[]{:S(2)}) collective-permute-start(bf16[256,128]{0,1:T(8,128)(2,1)} %collective-permute-done), channel_id=1, source_target_pairs={{0,1},{1,2},{2,3},{3,0},{4,5},{5,6},{6,7},{7,4},{8,9},{9,10},{10,1... | collective-permute-start | bytes 196616 | tf_op jit(solution)/shard_map/ppermute | solution.py:84
  339.2 13.3 %copy-start.3 = (pred[256,256]{0,1:T(8,128)(4,1)S(1)}, pred[256,256]{0,1:T(8,128)(4,1)}, u32[]{:S(2)}) copy-start(pred[256,256]{0,1:T(8,128)(4,1)} %fusion.9) | copy-start | bytes 196612
  342.2 6.4 %collective-permute-start.2 = (bf16[256,128]{0,1:T(8,128)(2,1)}, bf16[256,128]{0,1:T(8,128)(2,1)S(1)}, u32[]{:S(2)}, u32[]{:S(2)}) collective-permute-start(bf16[256,128]{0,1:T(8,128)(2,1)} %collective-permute-done.1), channel_id=1, source_target_pairs={{0,1},{1,2},{2,3},{3,0},{4,5},{5,6},{6,7},{7,4},{8,9},{9,10},{10,1... | collective-permute-start | bytes 196616 | tf_op jit(solution)/shard_map/ppermute | solution.py:84
Sparse Core Ops, SparseCore 0:
  9.5 39.4 all-gather.3
  52.1 145.1 all-gather.5
  200.4 133.7 all-gather.7
